TPU v7x, 32 devices: a whole 2x2x4 slice. The times are simulated.
32 devices in a mesh: visit: 8 (over z, x), sky: 4 (over y, core).
Axes of the slice: x: 2, y: 2, z: 4, core: 2. Of those that a mesh axis runs over, the one named last changes fastest.
Arguments:
- warped: bfloat16 [16, 512, 2048], P('visit', 'sky'), may hold values from -11 to 21
- inv_var: bfloat16 [16, 512, 2048], P('visit', 'sky'), may hold values from 0.19921875 to 5
- intersection: int32 [8, 4, 4], P('visit', 'sky'), may hold values from 0 to 3, as said below
- col_start: int32 [8, 4], P('visit', 'sky'), may hold values from 0 to 1536, as said below
- row_interp: bfloat16 [8, 4, 512, 512], P('visit', 'sky'), may hold values from -0.22 to 1.4, as said below
- col_interp: bfloat16 [8, 4, 512, 512], P('visit', 'sky'), may hold values from -0.22 to 1.4, as said below
- cell_ids: int32 [8, 4, 4, 4], P('visit', 'sky'), may hold values from 0 to 15
- kernels: bfloat16 [8, 4, 16, 121], P('visit', 'sky'), may hold values from -0.59765625 to 0.59765625
- science: bfloat16 [8, 4, 512, 512], P('visit', 'sky'), may hold values from -8 to 8
- inv_sigma: bfloat16 [8, 4, 512, 512], P('visit', 'sky'), may hold values from 0.29882812 to 1
Outputs:
- coadd: float32 [512, 2048], P('sky')
- outlier_weight: float32 [8, 4, 512, 512], P('visit', 'sky')
Inputs may be any that keep to these rules, and one draw needn't show every extreme that they name: `intersection`: the 4 strip numbers of one tile are distinct. `col_start`: a multiple of 128. `row_interp`: nonzero only within two places of the diagonal, each row's diagonal entry larger than the sum of its other magnitudes. `col_interp`: nonzero only within two places of the diagonal, each row's diagonal entry larger than the sum of its other magnitudes.
All inputs are finite; a program needn't handle non-finite values.
Results may differ from a plain program's by a relative error of at most 0.0017.
Values may be sent and summed in bfloat16 or wider, within the bound.
No kernel may reach another device: no remote copies, remote signals or barrier semaphores. Data moves between devices by JAX's collectives and lax.ppermute only.
A program may use at most 64 MiB of HBM per device.

v0:
```python
import jax
import jax.numpy as jnp
from jax import lax
from jax.sharding import PartitionSpec as P

STRIP = 128
NOV = 4
TILE = 512
KSIZE = 11
CELL = 128
NCELL = 16
PASSES = 3
CAUCHY = 2.0
OUTLIER = 3.0


def local_coadd(warped_all, var_all):
    values = warped_all.astype(jnp.float32)
    weights = var_all.astype(jnp.float32)
    root_weight = jnp.sqrt(weights)
    coadd_field = jnp.sum(weights * values, axis=0) / jnp.sum(weights, axis=0)
    for pass_index in range(PASSES):
        scaled = (values - coadd_field[None]) * root_weight / CAUCHY
        cauchy = weights / (1.0 + scaled * scaled)
        coadd_field = jnp.sum(cauchy * values, axis=0) / jnp.sum(cauchy, axis=0)
    return coadd_field


def psf_match(blotted, cell_grid, kernel_table):
    tile_side = blotted.shape[1]
    blocks = tile_side // CELL
    half_width = KSIZE // 2
    window = CELL + KSIZE - 1
    picker = (cell_grid.reshape(-1)[:, None] == jnp.arange(NCELL, dtype=jnp.int32)[None, :]).astype(
        jnp.bfloat16
    )
    tap_rows = jnp.dot(picker, kernel_table, preferred_element_type=jnp.float32)
    tap_rows = tap_rows.reshape(blocks, blocks, KSIZE, KSIZE)
    source = jnp.arange(window, dtype=jnp.int32)[:, None]
    target = jnp.arange(CELL, dtype=jnp.int32)[None, :]
    diagonal = (
        (source - target)[None] == jnp.arange(KSIZE, dtype=jnp.int32)[:, None, None]
    ).astype(jnp.float32)
    banded_all = jnp.einsum(
        "xyab,bcl->xyacl", tap_rows, diagonal, precision=lax.Precision.HIGHEST
    ).astype(jnp.bfloat16)
    padded = jnp.pad(blotted, ((half_width, half_width), (half_width, half_width)))
    row_parts = []
    for row_block in range(blocks):
        rows_window = lax.slice_in_dim(padded, row_block * CELL, row_block * CELL + window, axis=0)
        col_parts = []
        for col_block in range(blocks):
            cols_window = lax.slice_in_dim(
                rows_window, col_block * CELL, col_block * CELL + window, axis=1
            )
            horizontal = jnp.einsum(
                "rc,acl->arl",
                cols_window,
                banded_all[row_block, col_block],
                preferred_element_type=jnp.float32,
            )
            summed = horizontal[0, 0:CELL, :]
            for tap_row in range(1, KSIZE):
                summed = summed + horizontal[tap_row, tap_row : tap_row + CELL, :]
            col_parts.append(summed)
        row_parts.append(jnp.concatenate(col_parts, axis=1))
    return jnp.concatenate(row_parts, axis=0)


def shards(
    warped,
    inv_var,
    intersection,
    col_start,
    row_interp,
    col_interp,
    cell_ids,
    kernels,
    science,
    inv_sigma,
):
    warped_all, var_all = (
        lax.all_to_all(warped, "visit", split_axis=2, concat_axis=0, tiled=True),
        lax.all_to_all(inv_var, "visit", split_axis=2, concat_axis=0, tiled=True),
    )
    column_share = local_coadd(warped_all, var_all)
    coadd_field = lax.all_gather(column_share, "visit", axis=1, tiled=True)
    coadd_low = coadd_field.astype(jnp.bfloat16)
    strips = intersection[0, 0]
    start_col = col_start[0, 0]
    rows_map = row_interp[0, 0]
    shard_rows = lax.all_gather(coadd_low, "sky", axis=0, tiled=True)
    first_row = jnp.int32(0)
    row_count = shard_rows.shape[0]
    block_rows = min(row_count, STRIP)
    total = jnp.zeros((TILE, TILE), jnp.float32)
    for block_index in range(row_count // block_rows):
        block_first = first_row + block_index * block_rows
        strip_of = block_first // STRIP
        inside = block_first % STRIP
        matches = strips == strip_of
        slot_index = jnp.sum(jnp.where(matches, jnp.arange(NOV, dtype=jnp.int32), 0))
        present = jnp.any(matches)
        block_data = shard_rows[block_index * block_rows : (block_index + 1) * block_rows]

        def add_block(current):
            chosen = lax.dynamic_slice_in_dim(rows_map, slot_index * STRIP + inside, block_rows, 1)
            columns = lax.dynamic_slice_in_dim(block_data, start_col, TILE, 1)
            return current + jnp.dot(chosen, columns, preferred_element_type=jnp.float32)

        total = lax.cond(present, add_block, lambda current: current, total)
    blotted = jnp.dot(
        total.astype(jnp.bfloat16), col_interp[0, 0], preferred_element_type=jnp.float32
    ).astype(jnp.bfloat16)
    matched = psf_match(blotted, cell_ids[0, 0], kernels[0, 0])
    residual = (
        (science[0, 0].astype(jnp.float32) - matched)
        * inv_sigma[0, 0].astype(jnp.float32)
        / OUTLIER
    )
    outlier = 1.0 / (1.0 + residual * residual)
    return (coadd_field, outlier[None, None])


def solution(mesh):
    in_specs = (
        P("visit", "sky", None),
        P("visit", "sky", None),
        P("visit", "sky", None),
        P("visit", "sky"),
        P("visit", "sky", None, None),
        P("visit", "sky", None, None),
        P("visit", "sky", None, None),
        P("visit", "sky", None, None),
        P("visit", "sky", None, None),
        P("visit", "sky", None, None),
    )
    out_specs = (P("sky", None), P("visit", "sky", None, None))
    return jax.shard_map(shards, mesh=mesh, in_specs=in_specs, out_specs=out_specs, check_vma=False)
```

profile of v0, /device:TPU:0, one launch (start us, length us, event | category | flops | bytes accessed | tf_op | source)
XLA Modules:
  0.0 203.1 jit_solution(12061333700261532114)
XLA Ops:
  7.2 3.8 %copy.119 = bf16[2,128,2048]{1,0,2:T(2,128)(2,1)} copy(bf16[2,128,2048]{2,1,0:T(8,128)(2,1)} %param.18) | data formatting | bytes 2097152 | tf_op args[0]
  11.0 7.3 %all-to-all-start.1 = ((bf16[2,128,2048]{1,0,2:T(2,128)(2,1)}), bf16[2,128,2048]{1,0,2:T(2,128)(2,1)S(1)}, u32[]{:S(2)}, u32[]{:S(2)}) async-start(bf16[2,128,2048]{1,0,2:T(2,128)(2,1)} %copy.119), calls=%async_computation.1 | async-start | bytes 2097152 | tf_op jit(solution)/shard_map/all_to_all | solution.py:83
  18.3 2.0 copy.116
  20.3 23.8 %all-to-all-done.1 = bf16[2,128,2048]{1,0,2:T(2,128)(2,1)S(1)} async-done(((bf16[2,128,2048]{1,0,2:T(2,128)(2,1)}), bf16[2,128,2048]{1,0,2:T(2,128)(2,1)S(1)}, u32[]{:S(2)}, u32[]{:S(2)}) %all-to-all-start.1) | async-done | bytes 1048608 | tf_op jit(solution)/shard_map/all_to_all | solution.py:83
  44.0 4.2 %all-to-all-start = ((bf16[2,128,2048]{1,0,2:T(2,128)(2,1)}), bf16[2,128,2048]{1,0,2:T(2,128)(2,1)}, u32[]{:S(2)}, u32[]{:S(2)}) async-start(bf16[2,128,2048]{1,0,2:T(2,128)(2,1)} %copy.116), calls=%async_computation | async-start | bytes 2097152 | tf_op jit(solution)/shard_map/all_to_all | solution.py:84
  48.3 1.1 copy.120
  49.4 1.5 copy.121
  50.9 22.9 %all-to-all-done = bf16[2,128,2048]{1,0,2:T(2,128)(2,1)} async-done(((bf16[2,128,2048]{1,0,2:T(2,128)(2,1)}), bf16[2,128,2048]{1,0,2:T(2,128)(2,1)}, u32[]{:S(2)}, u32[]{:S(2)}) %all-to-all-start) | async-done | bytes 1048608 | tf_op jit(solution)/shard_map/all_to_all | solution.py:84
  73.8 2.3 %copy.117 = bf16[2,128,2048]{1,2,0:T(8,128)(2,1)} copy(bf16[2,128,2048]{1,0,2:T(2,128)(2,1)} %all-to-all-done) | data formatting | bytes 2097152 | tf_op jit(solution)/shard_map/all_to_all | solution.py:84
  76.2 2.6 %copy.118 = f32[2,128,8,256]{3,1,0,2:T(8,128)} copy(bf16[2,128,8,256]{1,3,2,0:T(8,128)(2,1)} %bitcast.283) | data formatting | bytes 3145728 | tf_op jit(solution)/shard_map/convert_element_type | solution.py:19
  78.8 2.0 %bitcast_reduce_fusion = (f32[128,256]{1,0:T(8,128)S(1)}, f32[128,256]{1,0:T(8,128)S(1)}) fusion(f32[2,128,8,256]{3,1,0,2:T(8,128)} %copy.118, f32[2,128,8,256]{3,1,0,2:T(8,128)S(1)} %copy.121), kind=kLoop, calls=%fused_computation.52 | loop fusion | flops 1507328 | bytes 4456448 | tf_op jit(solution)/shard_map/reduce_sum | solution.py:21
  81.0 1.2 fusion.106
  82.2 1.2 fusion.105
  83.5 1.2 fusion.104
  85.0 0.7 div.72
  85.7 39.2 %all-gather.3.cloned.1.call-done = f32[128,2048]{0,1:T(8,128)} async-done(((f32[128,256]{0,1:T(8,128)}), f32[128,2048]{0,1:T(8,128)}) %all-gather.3.cloned.1.call-update) | async-done | bytes 1048592 | tf_op jit(solution)/shard_map/all_gather | solution.py:87
  124.9 2.1 %convert_element_type.88 = bf16[128,2048]{0,1:T(8,128)(2,1)} convert(f32[128,2048]{0,1:T(8,128)} %all-gather.3.cloned.1.call-done) | non-fusion elementwise | flops 262144 | bytes 1572864 | tf_op jit(solution)/shard_map/convert_element_type | solution.py:88
  127.0 0.7 fusion.125
  130.9 7.5 %convolution_convert_fusion = bf16[4,4,11,138,128]{4,2,3,1,0:T(8,128)(2,1)S(1)} fusion(s32[138,128]{1,0:T(8,128)S(1)} %iota_subtract_fusion, f32[4,4,11,11,1]{3,1,2,0,4:T(4,128)S(1)} %convolution_bitcast_fusion.16), kind=kOutput, calls=%fused_computation.24 | convolution fusion | flops 413673216 | bytes 6296128 | tf_op jit(solution)/shard_map/xyab,bcl->xyacl/dot_general | solution.py:44
  138.4 3.4 %slice_bitcast_fusion.15 = (bf16[11,138,128]{2,0,1:T(8,128)(2,1)}, bf16[11,138,128]{2,0,1:T(8,128)(2,1)}, bf16[11,138,128]{2,0,1:T(8,128)(2,1)}, bf16[11,138,128...) fusion(bf16[4,4,11,138,128]{4,2,3,1,0:T(8,128)(2,1)S(1)} %convo, ...), kind=kLoop, calls=%fused_computation.106 | loop fusion | bytes 12435456 | tf_op jit(solution)/shard_map/squeeze | solution.py:59
  141.8 1.3 copy.146
  143.1 5.7 %all-gather.5.cloned.1.call-done = bf16[512,2048]{0,1:T(8,128)(2,1)} async-done(((bf16[128,2048]{0,1:T(8,128)(2,1)}), bf16[512,2048]{0,1:T(8,128)(2,1)}) %all-gather.5.cloned.1.call-update) | async-done | bytes 2097168 | tf_op jit(solution)/shard_map/all_gather | solution.py:92
  148.7 7.5 %conditional.4 = (f32[512,512]{1,0:T(8,128)S(1)}) conditional(s32[]{:T(128)} %convert_element_type.87, () %tuple.44, (pred[1,1,4]{2,1,0:T(4,128)(4,1)S(1)}, bf16[512,512]{1,0:T(8,128)(2,1)}, s32[]{:T(128)}, bf16[512,2048]{0,1:T(8,128)(2,1)}, s32[]{:T(128)}, /*index=5*/s32[4]{0:T(128)S(1)}, s32[4]{0:T(128)S(1)}) %tuple.105), branch_computations={%region_13.14_spmd, %region_14.15_spmd} | conditional | flops 67108880 | bytes 6553740 | solution.py:111
  150.7 0.7 fusion.3
  152.0 2.9 %copy.126 = bf16[512,2048]{1,0:T(8,128)(2,1)S(1)} copy(bf16[512,2048]{0,1:T(8,128)(2,1)} %get-tuple-element.197) | data formatting | bytes 4194304 | tf_op jit(solution)/shard_map
  155.0 1.3 fusion
  156.3 9.5 %conditional.5 = (f32[512,512]{1,0:T(8,128)S(1)}) conditional(s32[]{:T(128)} %convert_element_type.86, f32[512,512]{1,0:T(8,128)S(1)} %get-tuple-element.261, (pred[1,1,4]{2,1,0:T(4,128)(4,1)S(1)}, bf16[512,512]{1,0:T(8,128)(2,1)}, s32[]{:T(128)}, bf16[512,2048]{0,1:T(8,128)(2,1)}, f32[512,512]{1,0:T(8,128)S(1)}, /*index=5*/s32[]{:T(128)}, ...), branch_computations={%region_16.17_spmd, %region_17.18_spmd} | conditional | flops 67371024 | bytes 7602316 | solution.py:111
  158.2 0.6 fusion.7
  159.4 4.0 %copy.127 = bf16[512,2048]{1,0:T(8,128)(2,1)} copy(bf16[512,2048]{0,1:T(8,128)(2,1)} %get-tuple-element.204) | data formatting | bytes 4194304 | tf_op jit(solution)/shard_map
  163.4 1.1 slice.877
  164.5 1.3 convolution_add_fusion
  165.8 9.6 %conditional.6 = (f32[512,512]{1,0:T(8,128)S(1)}) conditional(s32[]{:T(128)} %convert_element_type.85, f32[512,512]{1,0:T(8,128)S(1)} %get-tuple-element.262, (pred[1,1,4]{2,1,0:T(4,128)(4,1)S(1)}, bf16[512,512]{1,0:T(8,128)(2,1)}, s32[]{:T(128)}, bf16[512,2048]{0,1:T(8,128)(2,1)}, f32[512,512]{1,0:T(8,128)S(1)}, /*index=5*/s32[]{:T(128)}, ...), branch_computations={%region_19.20_spmd, %region_20.21_spmd} | conditional | flops 67371024 | bytes 7602316 | solution.py:111
  167.9 0.6 fusion.11
  169.1 4.0 %copy.128 = bf16[512,2048]{1,0:T(8,128)(2,1)} copy(bf16[512,2048]{0,1:T(8,128)(2,1)} %get-tuple-element.212) | data formatting | bytes 4194304 | tf_op jit(solution)/shard_map
  173.0 1.1 slice.878
  174.1 1.3 convolution_add_fusion.1
  175.4 9.4 %conditional.7 = (f32[512,512]{1,0:T(8,128)S(1)}) conditional(s32[]{:T(128)} %convert_element_type.84, f32[512,512]{1,0:T(8,128)S(1)} %get-tuple-element.263, (pred[1,1,4]{2,1,0:T(4,128)(4,1)S(1)}, s32[4]{0:T(128)S(1)}, bf16[512,512]{1,0:T(8,128)(2,1)}, bf16[512,2048]{0,1:T(8,128)(2,1)}, s32[]{:T(128)}, /*index=5*/f32[512,512]{1,0:T(8,128)S(1)}) %tuple.108), branch_computations={%region_21.22_spmd, %region_22.24_spmd} | conditional | flops 67371024 | bytes 7602296 | solution.py:111
  177.4 0.6 fusion.15
  178.5 4.0 %copy.129 = bf16[512,2048]{1,0:T(8,128)(2,1)} copy(bf16[512,2048]{0,1:T(8,128)(2,1)} %get-tuple-element.220) | data formatting | bytes 4194304 | tf_op jit(solution)/shard_map
  182.5 1.1 slice.879
  183.6 1.3 convolution_add_fusion.2
  184.9 0.4 convolution_convert_fusion.1
  185.3 0.6 copy-done.17
  188.5 0.3 convolution_bitcast_fusion.4
  192.3 0.3 convolution_bitcast_fusion.11
  193.8 0.3 convolution_bitcast_fusion.14
  194.3 0.5 copy-done.19
  195.0 1.3 fusion.42
  (96 shorter events, 8.4 us)
Async XLA Ops:
  7.2 177.7 %copy-start = (bf16[1,1,512,512]{3,2,1,0:T(8,128)(2,1)S(1)}, bf16[1,1,512,512]{3,2,1,0:T(8,128)(2,1)}, u32[]{:S(2)}) copy-start(bf16[1,1,512,512]{3,2,1,0:T(8,128)(2,1)} %param.23) | copy-start | bytes 1572868
  7.2 11.1 %copy-start.18 = (bf16[2,128,2048]{2,1,0:T(8,128)(2,1)S(1)}, bf16[2,128,2048]{2,1,0:T(8,128)(2,1)}, u32[]{:S(2)}) copy-start(bf16[2,128,2048]{2,1,0:T(8,128)(2,1)} %param.19) | copy-start | bytes 3145732
  11.0 33.0 %all-to-all-start.1 = ((bf16[2,128,2048]{1,0,2:T(2,128)(2,1)}), bf16[2,128,2048]{1,0,2:T(2,128)(2,1)S(1)}, u32[]{:S(2)}, u32[]{:S(2)}) async-start(bf16[2,128,2048]{1,0,2:T(2,128)(2,1)} %copy.119), calls=%async_computation.1 | async-start | bytes 2097152 | tf_op jit(solution)/shard_map/all_to_all | solution.py:83
  44.0 29.8 %all-to-all-start = ((bf16[2,128,2048]{1,0,2:T(2,128)(2,1)}), bf16[2,128,2048]{1,0,2:T(2,128)(2,1)}, u32[]{:S(2)}, u32[]{:S(2)}) async-start(bf16[2,128,2048]{1,0,2:T(2,128)(2,1)} %copy.116), calls=%async_computation | async-start | bytes 2097152 | tf_op jit(solution)/shard_map/all_to_all | solution.py:84
  48.3 76.7 %all-gather.3.cloned.1.call-start = ((), (), s32[]{:S(2)}) async-start(), calls=%async_computation.2 | async-start | bytes 1179648 | tf_op jit(solution)/shard_map/all_gather | solution.py:87
  78.8 2.2 %copy-start.1 = (f32[2,128,8,256]{3,1,0,2:T(8,128)S(1)}, f32[2,128,8,256]{3,1,0,2:T(8,128)}, u32[]{:S(2)}) copy-start(f32[2,128,8,256]{3,1,0,2:T(8,128)} %copy.118) | copy-start | bytes 6291460
  84.7 42.3 %copy-start.23 = (s32[1,1,4]{2,1,0:T(1,128)S(1)}, s32[1,1,4]{2,1,0:T(1,128)}, u32[]{:S(2)}) copy-start(s32[1,1,4]{2,1,0:T(1,128)} %param.20) | copy-start | bytes 52
  84.7 45.6 %copy-start.21 = (bf16[1,1,16,121]{3,2,1,0:T(8,128)(2,1)S(1)}, bf16[1,1,16,121]{3,2,1,0:T(8,128)(2,1)}, u32[]{:S(2)}) copy-start(bf16[1,1,16,121]{3,2,1,0:T(8,128)(2,1)} %param.25) | copy-start | bytes 11620
  84.7 45.9 %copy-start.22 = (s32[1,1,4,4]{3,2,1,0:T(4,128)S(1)}, s32[1,1,4,4]{3,2,1,0:T(4,128)}, u32[]{:S(2)}) copy-start(s32[1,1,4,4]{3,2,1,0:T(4,128)} %param.24) | copy-start | bytes 196
  85.7 63.1 %all-gather.5.cloned.1.call-start = ((), (), s32[]{:S(2)}) async-start(), calls=%async_computation.3 | async-start | bytes 2621440 | tf_op jit(solution)/shard_map/all_gather | solution.py:92
  138.4 3.4 %copy-start.2 = (f32[128,2048]{0,1:T(8,128)S(1)}, f32[128,2048]{0,1:T(8,128)}, u32[]{:S(2)}) copy-start(f32[128,2048]{0,1:T(8,128)} %all-gather.3.cloned.1.call-done) | copy-start | bytes 3145732
  184.9 1.1 copy-start.17
  184.9 1.4 copy-start.16
  185.9 1.1 copy-start.15
  186.3 1.1 copy-start.14
  187.0 1.1 copy-start.13
  187.4 1.1 copy-start.12
  188.1 1.1 copy-start.11
  188.5 1.1 copy-start.10
  189.0 1.1 copy-start.9
  189.6 1.1 copy-start.8
  190.1 1.1 copy-start.7
  190.7 1.1 copy-start.6
  191.1 1.1 copy-start.5
  191.8 1.1 copy-start.4
  192.3 1.1 copy-start.3
  193.8 1.0 copy-start.19
  193.8 1.2 copy-start.20
Sparse Core Ops, SparseCore 0:
  85.8 39.1 all-gather.2
  127.2 21.5 all-gather.4
where the time goes:
time: 204 us; the launch traced here: 203 us
  waiting for transfers between devices  91.6 us (45%)
  local copies, waits for them, and re-layouts  39.7 us (19%)
  matrix products  18.5 us (9%)
  between operations  17.1 us (8%)
  other arithmetic  14.2 us (7%)
  starting transfers between devices  11.6 us (6%)
  loops' own time  10.3 us (5%)
    all_gather x1, waiting for transfers between devices, shards(): coadd_field = lax.all_gather(column_share, 'visit', axis=1, tiled=True)  39.2 us
    all_to_all x1, waiting for transfers between devices, shards(): lax.all_to_all(warped, 'visit', split_axis=2, concat_axis=0, tiled=True)  23.8 us
    all_to_all x1, waiting for transfers between devices, shards(): lax.all_to_all(inv_var, 'visit', split_axis=2, concat_axis=0, tiled=True)  22.9 us
    another operation x4, local copies, waits for them, and re-layouts  14.8 us
    unnamed x53, local copies, waits for them, and re-layouts  10.5 us
    another operation x4, loops' own time, shards(): total = lax.cond(present, add_block, lambda current: current, total)  10.3 us
    dot_general x1, matrix products, psf_match(): jnp.einsum('xyab,bcl->xyacl', tap_rows, diagonal, precision=lax.Precision...  7.51 us
    all_to_all x1, starting transfers between devices, shards(): lax.all_to_all(warped, 'visit', split_axis=2, concat_axis=0, tiled=True)  7.28 us
  transfers between devices with their start and end apart: 4, of which 4 were waited for; matrix products, arithmetic and copies ran while one was open for 9% of the time, Pallas kernels for 0%

commit v1 on v0

--- a/solution.py
+++ b/solution.py
@@ -1,3 +1,4 @@
+import functools
 import jax
 import jax.numpy as jnp
 from jax import lax
@@ -12,6 +13,38 @@
 PASSES = 3
 CAUCHY = 2.0
 OUTLIER = 3.0
+
+
+def bind_links(frame, row_dim, view):
+    ready = frame.shape
+    m_next = frame.reshape(*ready[:row_dim], view, ready[row_dim] // view, *ready[row_dim + 1 :])
+    return jnp.moveaxis(m_next, row_dim, 0)
+
+
+def choose_panels(v0, d_out):
+    v0 = jnp.moveaxis(v0, 0, d_out)
+    block_last = v0.shape
+    return v0.reshape(
+        *block_last[:d_out], block_last[d_out] * block_last[d_out + 1], *block_last[d_out + 2 :]
+    )
+
+
+def track_hubs_now(here_x, named_axis, block_in, x_local):
+    current_value, carry_out = (lax.axis_size(named_axis), lax.axis_index(named_axis))
+    reply = bind_links(here_x, block_in, current_value)
+    u = 1
+    copies = [reply[carry_out]]
+    while u < current_value:
+        state_now = reply[carry_out ^ u]
+        copies.append(
+            lax.ppermute(state_now, named_axis, [(w, w ^ u) for w in range(current_value)])
+        )
+        u += 1
+    reply = jnp.stack(copies)[carry_out ^ jnp.arange(current_value)]
+    return choose_panels(reply, x_local)
+
+
+set_cells_in = functools.partial(track_hubs_now, named_axis="visit", block_in=2, x_local=0)
 
 
 def local_coadd(warped_all, var_all):
@@ -81,7 +114,7 @@
 ):
     warped_all, var_all = (
         lax.all_to_all(warped, "visit", split_axis=2, concat_axis=0, tiled=True),
-        lax.all_to_all(inv_var, "visit", split_axis=2, concat_axis=0, tiled=True),
+        set_cells_in(inv_var),
     )
     column_share = local_coadd(warped_all, var_all)
     coadd_field = lax.all_gather(column_share, "visit", axis=1, tiled=True)

time: 204 us -> 182 us (0.89)
  waiting for transfers between devices: 91.6 us -> 64.9 us
  starting transfers between devices: 11.6 us -> 25.6 us
  local copies, waits for them, and re-layouts: 39.7 us -> 29.2 us
    all_to_all x1, waiting for transfers between devices: 23.8 us -> 0.01 us  [shards(): lax.all_to_all(warped, 'visit', split_axis=2, concat_axis=0, tiled=True)]
    all_to_all x1 -> x0, waiting for transfers between devices: 22.9 us -> none  [shards(): lax.all_to_all(inv_var, 'visit', split_axis=2, concat_axis=0, tiled=True)]
    ppermute x0 -> x7, starting transfers between devices: none -> 18.2 us  [track_hubs_now(): lax.ppermute(state_now, named_axis, [(w, w ^ u) for w in range(current_va...]
    ppermute x0 -> x7, waiting for transfers between devices: none -> 16.2 us  [track_hubs_now(): lax.ppermute(state_now, named_axis, [(w, w ^ u) for w in range(current_va...]
    another operation x4 -> x10, local copies, waits for them, and re-layouts: 14.8 us -> 4.53 us
    all_to_all x1 -> x0, starting transfers between devices: 4.24 us -> none  [shards(): lax.all_to_all(inv_var, 'visit', split_axis=2, concat_axis=0, tiled=True)]
    convert_element_type x1 -> x0, local copies, waits for them, and re-layouts: 2.59 us -> none  [local_coadd(): weights = var_all.astype(jnp.float32)]
    all_to_all x1 -> x0, local copies, waits for them, and re-layouts: 2.33 us -> none  [shards(): lax.all_to_all(inv_var, 'visit', split_axis=2, concat_axis=0, tiled=True)]
  transfers between devices with their start and end apart: 4 -> 10, of which waited for: 4 -> 5; matrix products, arithmetic and copies ran while one was open for 9% -> 13% of each run, Pallas kernels for 0% -> 0%
where the time goes in v1:
time: 182 us; the launch traced here: 181 us
  waiting for transfers between devices  64.9 us (36%)
  local copies, waits for them, and re-layouts  29.2 us (16%)
  starting transfers between devices  25.6 us (14%)
  matrix products  18.5 us (10%)
  between operations  17.2 us (9%)
  other arithmetic  14.3 us (8%)
  loops' own time  10.8 us (6%)
    all_gather x1, waiting for transfers between devices, shards(): coadd_field = lax.all_gather(column_share, 'visit', axis=1, tiled=True)  41.4 us
    ppermute x7, starting transfers between devices, track_hubs_now(): lax.ppermute(state_now, named_axis, [(w, w ^ u) for w in range(current_va...  18.2 us
    ppermute x7, waiting for transfers between devices, track_hubs_now(): lax.ppermute(state_now, named_axis, [(w, w ^ u) for w in range(current_va...  16.2 us
    unnamed x52, local copies, waits for them, and re-layouts  12.8 us
    another operation x4, loops' own time, shards(): total = lax.cond(present, add_block, lambda current: current, total)  10.8 us
    dot_general x1, matrix products, psf_match(): jnp.einsum('xyab,bcl->xyacl', tap_rows, diagonal, precision=lax.Precision...  7.48 us
    all_to_all x1, starting transfers between devices, shards(): lax.all_to_all(warped, 'visit', split_axis=2, concat_axis=0, tiled=True)  7.28 us
    all_gather x1, waiting for transfers between devices, shards(): shard_rows = lax.all_gather(coadd_low, 'sky', axis=0, tiled=True)  7.24 us
  transfers between devices with their start and end apart: 10, of which 5 were waited for; matrix products, arithmetic and copies ran while one was open for 13% of the time, Pallas kernels for 0%

profile of v1, /device:TPU:0, one launch (start us, length us, event | category | flops | bytes accessed | tf_op | source)
XLA Modules:
  0.0 180.5 jit_solution(9944696654322616430)
XLA Ops:
  7.2 3.7 %copy.82 = bf16[2,128,2048]{1,0,2:T(2,128)(2,1)} copy(bf16[2,128,2048]{2,1,0:T(8,128)(2,1)} %param.18) | data formatting | bytes 2097152 | tf_op args[0]
  10.9 7.3 %all-to-all-start = ((bf16[2,128,2048]{1,0,2:T(2,128)(2,1)}), bf16[2,128,2048]{1,0,2:T(2,128)(2,1)S(1)}, u32[]{:S(2)}, u32[]{:S(2)}) async-start(bf16[2,128,2048]{1,0,2:T(2,128)(2,1)} %copy.82), calls=%async_computation | async-start | bytes 2097152 | tf_op jit(solution)/shard_map/all_to_all | solution.py:116
  18.3 1.6 copy.73
  19.9 0.8 constant_dynamic-slice_fusion
  20.7 1.7 copy.75
  22.3 1.9 %collective-permute-start = (bf16[2,128,256]{2,1,0:T(8,128)(2,1)}, bf16[2,128,256]{2,1,0:T(8,128)(2,1)}, u32[]{:S(2)}, u32[]{:S(2)}) collective-permute-start(bf16[2,128,256]{2,1,0:T(8,128)(2,1)} %bitcast.6), channel_id=1, source_target_pairs={{0,4},{4,0},{8,12},{12,8},{16,20},{20,16},{24,28},{28,24},{1,5},{5... | collective-permute-start | bytes 393224 | tf_op jit(solution)/shard_map/ppermute | solution.py:40
  24.3 0.8 copy.76
  25.1 1.5 collective-permute-start.1
  26.5 0.8 copy.77
  27.5 2.9 %collective-permute-start.3 = (bf16[2,128,256]{2,1,0:T(8,128)(2,1)S(1)}, bf16[2,128,256]{2,1,0:T(8,128)(2,1)}, u32[]{:S(2)}, u32[]{:S(2)}) collective-permute-start(bf16[2,128,256]{2,1,0:T(8,128)(2,1)S(1)} %bitcast.263), channel_id=1, source_target_pairs={{0,16},{4,20},{8,24},{12,28},{16,0},{20,4},{24,8},{28,12},{1,17},{... | collective-permute-start | bytes 393224 | tf_op jit(solution)/shard_map/ppermute | solution.py:40
  30.5 1.5 collective-permute-start.4
  32.5 5.7 %collective-permute-start.5 = (bf16[2,128,256]{2,1,0:T(8,128)(2,1)S(1)}, bf16[2,128,256]{2,1,0:T(8,128)(2,1)S(1)}, u32[]{:S(2)}, u32[]{:S(2)}) collective-permute-start(bf16[2,128,256]{2,1,0:T(8,128)(2,1)S(1)} %bitcast.264), channel_id=1, source_target_pairs={{0,24},{4,28},{8,16},{12,20},{16,8},{20,12},{24,0},{28,4},{1,25},{... | collective-permute-start | bytes 393224 | tf_op jit(solution)/shard_map/ppermute | solution.py:40
  38.2 0.9 bitcast_dynamic-update-slice_fusion.6
  39.4 4.6 %collective-permute-start.6 = (bf16[2,128,256]{2,1,0:T(8,128)(2,1)S(1)}, bf16[2,128,256]{2,1,0:T(8,128)(2,1)S(1)}, u32[]{:S(2)}, u32[]{:S(2)}) collective-permute-start(bf16[2,128,256]{2,1,0:T(8,128)(2,1)S(1)} %bitcast.261), channel_id=1, source_target_pairs={{0,28},{4,24},{8,20},{12,16},{16,12},{20,8},{24,4},{28,0},{1,29},{... | collective-permute-start | bytes 393224 | tf_op jit(solution)/shard_map/ppermute | solution.py:40
  44.0 0.9 bitcast_dynamic-update-slice_fusion.5
  44.9 0.9 bitcast_dynamic-update-slice_fusion.4
  45.8 13.7 %collective-permute-done.3 = bf16[2,128,256]{2,1,0:T(8,128)(2,1)} collective-permute-done((bf16[2,128,256]{2,1,0:T(8,128)(2,1)S(1)}, bf16[2,128,256]{2,1,0:T(8,128)(2,1)}, u32[]{:S(2)}, u32[]{:S(2)}) %collective-permute-start.3) | collective-permute-done | bytes 131104 | tf_op jit(solution)/shard_map/ppermute | solution.py:40
  59.5 0.9 bitcast_dynamic-update-slice_fusion.3
  60.4 2.3 %collective-permute-done.4 = bf16[2,128,256]{2,1,0:T(8,128)(2,1)S(1)} collective-permute-done((bf16[2,128,256]{2,1,0:T(8,128)(2,1)S(1)}, bf16[2,128,256]{2,1,0:T(8,128)(2,1)S(1)}, u32[]{:S(2)}, u32[]{:S(2)}) %collective-permute-start.4) | collective-permute-done | bytes 131104 | tf_op jit(solution)/shard_map/ppermute | solution.py:40
  62.7 1.6 gather_fusion
  64.3 1.1 copy.83
  65.4 1.5 copy.84
  66.9 1.6 convert_reduce_fusion
  68.6 1.3 fusion.40
  69.9 1.3 fusion.41
  71.2 1.3 fusion.42
  73.3 41.4 %all-gather.3.cloned.1.call-done = f32[128,2048]{1,0:T(8,128)} async-done(((f32[128,256]{1,0:T(8,128)}), f32[128,2048]{1,0:T(8,128)}) %all-gather.3.cloned.1.call-update) | async-done | bytes 1048592 | tf_op jit(solution)/shard_map/all_gather | solution.py:120
  114.7 2.1 %convert_element_type.80 = bf16[128,2048]{1,0:T(8,128)(2,1)} convert(f32[128,2048]{1,0:T(8,128)} %all-gather.3.cloned.1.call-done) | non-fusion elementwise | flops 262144 | bytes 1572864 | tf_op jit(solution)/shard_map/convert_element_type | solution.py:121
  116.8 0.7 fusion.123
  120.6 7.5 %convolution_convert_fusion = bf16[4,4,11,138,128]{4,2,3,1,0:T(8,128)(2,1)S(1)} fusion(s32[138,128]{1,0:T(8,128)S(1)} %iota_subtract_fusion, f32[4,4,11,11,1]{3,1,2,0,4:T(4,128)S(1)} %convolution_bitcast_fusion.16), kind=kOutput, calls=%fused_computation.25 | convolution fusion | flops 413673216 | bytes 6296128 | tf_op jit(solution)/shard_map/xyab,bcl->xyacl/dot_general | solution.py:77
  128.1 3.1 %slice_bitcast_fusion.15 = (bf16[11,138,128]{2,0,1:T(8,128)(2,1)}, bf16[11,138,128]{2,0,1:T(8,128)(2,1)}, bf16[11,138,128]{2,0,1:T(8,128)(2,1)}, bf16[11,138,128...) fusion(bf16[4,4,11,138,128]{4,2,3,1,0:T(8,128)(2,1)S(1)} %convo, ...), kind=kLoop, calls=%fused_computation.110 | loop fusion | bytes 12435456 | tf_op jit(solution)/shard_map/squeeze | solution.py:92
  131.3 7.2 %all-gather.5.cloned.1.call-done = bf16[512,2048]{1,0:T(8,128)(2,1)} async-done(((bf16[128,2048]{1,0:T(8,128)(2,1)}), bf16[512,2048]{1,0:T(8,128)(2,1)}) %all-gather.5.cloned.1.call-update) | async-done | bytes 2097168 | tf_op jit(solution)/shard_map/all_gather | solution.py:125
  138.5 5.7 %conditional.4 = (f32[512,512]{1,0:T(8,128)S(1)}) conditional(s32[]{:T(128)} %convert_element_type.79, () %tuple.44, (pred[1,1,4]{2,1,0:T(4,128)(4,1)S(1)}, bf16[512,512]{1,0:T(8,128)(2,1)}, s32[]{:T(128)}, bf16[512,2048]{1,0:T(8,128)(2,1)}, s32[]{:T(128)}, /*index=5*/s32[4]{0:T(128)S(1)}, s32[4]{0:T(128)S(1)}) %tuple.99), branch_computations={%region_13.14_spmd, %region_14.15_spmd} | conditional | flops 67108880 | bytes 2359436 | solution.py:144
  140.5 0.7 fusion.3
  141.9 1.1 slice.873
  142.9 1.3 fusion
  144.2 5.7 %conditional.5 = (f32[512,512]{1,0:T(8,128)S(1)}) conditional(s32[]{:T(128)} %convert_element_type.78, f32[512,512]{1,0:T(8,128)S(1)} %get-tuple-element.180, (pred[1,1,4]{2,1,0:T(4,128)(4,1)S(1)}, bf16[512,512]{1,0:T(8,128)(2,1)}, s32[]{:T(128)}, bf16[512,2048]{1,0:T(8,128)(2,1)}, f32[512,512]{1,0:T(8,128)S(1)}, /*index=5*/s32[]{:T(128)}, ...), branch_computations={%region_16.17_spmd, %region_17.18_spmd} | conditional | flops 67371024 | bytes 3408012 | solution.py:144
  146.2 0.7 fusion.7
  147.6 1.1 slice.874
  148.7 1.3 convolution_add_fusion
  150.0 5.9 %conditional.6 = (f32[512,512]{1,0:T(8,128)S(1)}) conditional(s32[]{:T(128)} %convert_element_type.77, f32[512,512]{1,0:T(8,128)S(1)} %get-tuple-element.181, (pred[1,1,4]{2,1,0:T(4,128)(4,1)S(1)}, bf16[512,512]{1,0:T(8,128)(2,1)}, s32[]{:T(128)}, bf16[512,2048]{1,0:T(8,128)(2,1)}, f32[512,512]{1,0:T(8,128)S(1)}, /*index=5*/s32[]{:T(128)}, ...), branch_computations={%region_19.20_spmd, %region_20.21_spmd} | conditional | flops 67371024 | bytes 3408012 | solution.py:144
  153.5 1.1 slice.875
  154.6 1.3 convolution_add_fusion.1
  155.9 5.7 %conditional.7 = (f32[512,512]{1,0:T(8,128)S(1)}) conditional(s32[]{:T(128)} %convert_element_type.76, f32[512,512]{1,0:T(8,128)S(1)} %get-tuple-element.182, (pred[1,1,4]{2,1,0:T(4,128)(4,1)S(1)}, s32[4]{0:T(128)S(1)}, bf16[512,512]{1,0:T(8,128)(2,1)}, bf16[512,2048]{1,0:T(8,128)(2,1)}, s32[]{:T(128)}, /*index=5*/f32[512,512]{1,0:T(8,128)S(1)}) %tuple.102), branch_computations={%region_21.22_spmd, %region_22.24_spmd} | conditional | flops 67371024 | bytes 3407992 | solution.py:144
  159.3 1.1 slice.450
  160.4 1.3 convolution_add_fusion.2
  171.5 1.3 fusion.39
  172.7 1.0 copy.158
  (114 shorter events, 13.4 us)
Async XLA Ops:
  7.2 154.5 %copy-start = (bf16[1,1,512,512]{3,2,1,0:T(8,128)(2,1)S(1)}, bf16[1,1,512,512]{3,2,1,0:T(8,128)(2,1)}, u32[]{:S(2)}) copy-start(bf16[1,1,512,512]{3,2,1,0:T(8,128)(2,1)} %param.23) | copy-start | bytes 1572868
  10.9 53.4 %all-to-all-start = ((bf16[2,128,2048]{1,0,2:T(2,128)(2,1)}), bf16[2,128,2048]{1,0,2:T(2,128)(2,1)S(1)}, u32[]{:S(2)}, u32[]{:S(2)}) async-start(bf16[2,128,2048]{1,0,2:T(2,128)(2,1)} %copy.82), calls=%async_computation | async-start | bytes 2097152 | tf_op jit(solution)/shard_map/all_to_all | solution.py:116
  18.2 96.5 %all-gather.3.cloned.1.call-start = ((), (), s32[]{:S(2)}) async-start(), calls=%async_computation.1 | async-start | bytes 1179648 | tf_op jit(solution)/shard_map/all_gather | solution.py:120
  22.3 10.1 %collective-permute-start = (bf16[2,128,256]{2,1,0:T(8,128)(2,1)}, bf16[2,128,256]{2,1,0:T(8,128)(2,1)}, u32[]{:S(2)}, u32[]{:S(2)}) collective-permute-start(bf16[2,128,256]{2,1,0:T(8,128)(2,1)} %bitcast.6), channel_id=1, source_target_pairs={{0,4},{4,0},{8,12},{12,8},{16,20},{20,16},{24,28},{28,24},{1,5},{5... | collective-permute-start | bytes 393224 | tf_op jit(solution)/shard_map/ppermute | solution.py:40
  25.1 14.3 %collective-permute-start.1 = (bf16[2,128,256]{2,1,0:T(8,128)(2,1)}, bf16[2,128,256]{2,1,0:T(8,128)(2,1)}, u32[]{:S(2)}, u32[]{:S(2)}) collective-permute-start(bf16[2,128,256]{2,1,0:T(8,128)(2,1)} %bitcast.8), channel_id=1, source_target_pairs={{0,8},{4,12},{8,0},{12,4},{16,24},{20,28},{24,16},{28,20},{1,9},{5... | collective-permute-start | bytes 393224 | tf_op jit(solution)/shard_map/ppermute | solution.py:40
  27.3 17.6 %collective-permute-start.2 = (bf16[2,128,256]{2,1,0:T(8,128)(2,1)}, bf16[2,128,256]{2,1,0:T(8,128)(2,1)}, u32[]{:S(2)}, u32[]{:S(2)}) collective-permute-start(bf16[2,128,256]{2,1,0:T(8,128)(2,1)} %bitcast.10), channel_id=1, source_target_pairs={{0,12},{4,8},{8,4},{12,0},{16,28},{20,24},{24,20},{28,16},{1,13},{... | collective-permute-start | bytes 393224 | tf_op jit(solution)/shard_map/ppermute | solution.py:40
  27.5 32.0 %collective-permute-start.3 = (bf16[2,128,256]{2,1,0:T(8,128)(2,1)S(1)}, bf16[2,128,256]{2,1,0:T(8,128)(2,1)}, u32[]{:S(2)}, u32[]{:S(2)}) collective-permute-start(bf16[2,128,256]{2,1,0:T(8,128)(2,1)S(1)} %bitcast.263), channel_id=1, source_target_pairs={{0,16},{4,20},{8,24},{12,28},{16,0},{20,4},{24,8},{28,12},{1,17},{... | collective-permute-start | bytes 393224 | tf_op jit(solution)/shard_map/ppermute | solution.py:40
  30.5 32.1 %collective-permute-start.4 = (bf16[2,128,256]{2,1,0:T(8,128)(2,1)S(1)}, bf16[2,128,256]{2,1,0:T(8,128)(2,1)S(1)}, u32[]{:S(2)}, u32[]{:S(2)}) collective-permute-start(bf16[2,128,256]{2,1,0:T(8,128)(2,1)S(1)} %bitcast.262), channel_id=1, source_target_pairs={{0,20},{4,16},{8,28},{12,24},{16,4},{20,0},{24,12},{28,8},{1,21},{... | collective-permute-start | bytes 393224 | tf_op jit(solution)/shard_map/ppermute | solution.py:40
  32.5 30.2 %collective-permute-start.5 = (bf16[2,128,256]{2,1,0:T(8,128)(2,1)S(1)}, bf16[2,128,256]{2,1,0:T(8,128)(2,1)S(1)}, u32[]{:S(2)}, u32[]{:S(2)}) collective-permute-start(bf16[2,128,256]{2,1,0:T(8,128)(2,1)S(1)} %bitcast.264), channel_id=1, source_target_pairs={{0,24},{4,28},{8,16},{12,20},{16,8},{20,12},{24,0},{28,4},{1,25},{... | collective-permute-start | bytes 393224 | tf_op jit(solution)/shard_map/ppermute | solution.py:40
  39.4 23.3 %collective-permute-start.6 = (bf16[2,128,256]{2,1,0:T(8,128)(2,1)S(1)}, bf16[2,128,256]{2,1,0:T(8,128)(2,1)S(1)}, u32[]{:S(2)}, u32[]{:S(2)}) collective-permute-start(bf16[2,128,256]{2,1,0:T(8,128)(2,1)S(1)} %bitcast.261), channel_id=1, source_target_pairs={{0,28},{4,24},{8,20},{12,16},{16,12},{20,8},{24,4},{28,0},{1,29},{... | collective-permute-start | bytes 393224 | tf_op jit(solution)/shard_map/ppermute | solution.py:40
  66.9 1.7 copy-start.1
  72.5 44.3 %copy-start.20 = (s32[1,1,4]{2,1,0:T(1,128)S(1)}, s32[1,1,4]{2,1,0:T(1,128)}, u32[]{:S(2)}) copy-start(s32[1,1,4]{2,1,0:T(1,128)} %param.20) | copy-start | bytes 52
  72.5 47.6 %copy-start.18 = (bf16[1,1,16,121]{3,2,1,0:T(8,128)(2,1)S(1)}, bf16[1,1,16,121]{3,2,1,0:T(8,128)(2,1)}, u32[]{:S(2)}) copy-start(bf16[1,1,16,121]{3,2,1,0:T(8,128)(2,1)} %param.25) | copy-start | bytes 11620
  72.5 47.8 %copy-start.19 = (s32[1,1,4,4]{3,2,1,0:T(4,128)S(1)}, s32[1,1,4,4]{3,2,1,0:T(4,128)}, u32[]{:S(2)}) copy-start(s32[1,1,4,4]{3,2,1,0:T(4,128)} %param.24) | copy-start | bytes 196
  73.2 65.3 %all-gather.5.cloned.1.call-start = ((), (), s32[]{:S(2)}) async-start(), calls=%async_computation.2 | async-start | bytes 2621440 | tf_op jit(solution)/shard_map/all_gather | solution.py:125
  161.7 1.1 copy-start.15
  161.7 1.5 copy-start.14
  162.7 1.1 copy-start.13
  163.1 1.1 copy-start.12
  163.8 1.1 copy-start.11
  164.2 1.1 copy-start.10
  164.9 1.1 copy-start.9
  165.3 1.1 copy-start.8
  165.8 1.1 copy-start.7
  166.4 1.1 copy-start.6
  166.9 1.1 copy-start.5
  167.5 1.1 copy-start.4
  167.9 1.1 copy-start.3
  170.3 1.0 copy-start.16
  170.3 1.2 copy-start.17
  170.7 2.0 %copy-start.2 = (f32[128,2048]{1,0:T(8,128)S(1)}, f32[128,2048]{1,0:T(8,128)}, u32[]{:S(2)}) copy-start(f32[128,2048]{1,0:T(8,128)} %all-gather.3.cloned.1.call-done) | copy-start | bytes 3145732
Sparse Core Ops, SparseCore 0:
  73.3 41.2 all-gather.2
  116.9 21.5 all-gather.4
